TPU v7x, 32 devices: a whole 2x2x4 slice. The times are simulated.
32 devices in a mesh: gx: 4 (over z), gy: 8 (over y, x, core).
Axes of the slice: x: 2, y: 2, z: 4, core: 2. Of those that a mesh axis runs over, the one named last changes fastest.
Arguments:
- forcing: float32 [2, 16, 64, 1024], P(None, None, 'gx', 'gy'), may hold values from -6 to 6
- viscosity: float32 [16, 64, 1024], P(None, 'gx', 'gy'), may hold values from 0.05 to 0.5
- observed: float32 [2, 64, 1024], P(None, 'gx', 'gy'), may hold values from -6 to 6
- beta_tiles: float32 [4, 128], P('gx', 'gy'), may hold values from 1 to 30
- ice_mask: int32 [64, 1024], P('gx', 'gy'), may hold values 0 or 1
- tile_owner: int32 [64, 1024], P('gx', 'gy'), may hold values from 0 to 127
Outputs:
- velocity: float32 [2, 16, 64, 1024], P(None, None, 'gx', 'gy')
- adjoint: float32 [2, 16, 64, 1024], P(None, None, 'gx', 'gy')
- grad_tiles: float32 [4, 128], P('gx', 'gy')
All inputs are finite; a program needn't handle non-finite values. No bound on the sum of `ice_mask` on one device may be relied on, other than what follows from the above.
Results may differ from a plain program's by a relative error of at most 0.000025.
Values sent between devices are 32-bit elements; how exact they have to be, the bound alone decides.
No kernel may reach another device: no remote copies, remote signals or barrier semaphores. Data moves between devices by JAX's collectives and lax.ppermute only.
A program may use at most 64 MiB of HBM per device.

v0:
```python
import jax
import jax.numpy as jnp
from jax import lax
from jax.sharding import PartitionSpec as P

PASSES = 4
OMEGA = 0.8
VERTICAL = 16.0
HALO = 2 * PASSES - 1


def with_halo(cells, sides, width):
    for axis, dim in sides:
        count = lax.axis_size(axis)
        ends = count - 1
        head = lax.slice_in_dim(cells, 0, width, axis=dim)
        tail = lax.slice_in_dim(cells, cells.shape[dim] - width, cells.shape[dim], axis=dim)
        cells = jnp.concatenate(
            [
                lax.ppermute(tail, axis, [(i, (i + 1) % count) for i in range(ends)]),
                cells,
                lax.ppermute(head, axis, [((i + 1) % count, i) for i in range(ends)]),
            ],
            axis=dim,
        )
    return cells


def lateral_terms(visc_pad):
    centre_visc = visc_pad[:, 1:-1, 1:-1]
    west_face = 0.5 * (centre_visc + visc_pad[:, :-2, 1:-1])
    east_face = 0.5 * (centre_visc + visc_pad[:, 2:, 1:-1])
    south_face = 0.5 * (centre_visc + visc_pad[:, 1:-1, :-2])
    north_face = 0.5 * (centre_visc + visc_pad[:, 1:-1, 2:])
    return (west_face, east_face, south_face, north_face)


def weights_xy():
    along_x = jnp.array([4.0, 1.0], jnp.float32).reshape(2, 1, 1, 1)
    along_y = jnp.array([1.0, 4.0], jnp.float32).reshape(2, 1, 1, 1)
    return (along_x, along_y)


def prepare(visc_pad, beta_col, ice_cover):
    faces = lateral_terms(visc_pad)
    west_face, east_face, south_face, north_face = faces
    along_x, along_y = weights_xy()
    centre_visc = visc_pad[:, 1:-1, 1:-1]
    vertical = VERTICAL * 0.5 * (centre_visc[:-1] + centre_visc[1:])
    zero_row = jnp.zeros_like(centre_visc[:1])
    upper_link = jnp.concatenate([vertical, zero_row], 0)
    lower_link = jnp.concatenate([zero_row, vertical], 0)
    basal = jnp.concatenate([jnp.zeros_like(centre_visc[:-1]), beta_col[None]], 0)
    diagonal = along_x * (west_face + east_face) + along_y * (south_face + north_face)
    diagonal = diagonal + upper_link + lower_link + basal + (1.0 - ice_cover)
    layer_count = visc_pad.shape[0]
    ratio_list = []
    inverse_list = []
    for layer_idx in range(layer_count):
        pivot = diagonal[:, layer_idx]
        if layer_idx > 0:
            pivot = pivot + lower_link[layer_idx] * ratio_list[-1]
        inverse = 1.0 / pivot
        inverse_list.append(inverse)
        ratio_list.append(-upper_link[layer_idx] * inverse)
    return (faces, lower_link, jnp.stack(ratio_list, 1), jnp.stack(inverse_list, 1))


def relax(vel_pad, rhs_field, faces, lower_link, ratios, inverses, ice_cover):
    west_face, east_face, south_face, north_face = faces
    along_x, along_y = weights_xy()
    lateral = along_x * (west_face * vel_pad[:, :, :-2, 1:-1] + east_face * vel_pad[:, :, 2:, 1:-1])
    lateral = lateral + along_y * (
        south_face * vel_pad[:, :, 1:-1, :-2] + north_face * vel_pad[:, :, 1:-1, 2:]
    )
    right_side = rhs_field + lateral
    layer_count = right_side.shape[1]
    forward_list = []
    for layer_idx in range(layer_count):
        value = right_side[:, layer_idx]
        if layer_idx > 0:
            value = value + lower_link[layer_idx] * forward_list[-1]
        forward_list.append(value * inverses[:, layer_idx])
    solved = [None] * layer_count
    solved[layer_count - 1] = forward_list[layer_count - 1]
    for layer_idx in range(layer_count - 2, -1, -1):
        solved[layer_idx] = forward_list[layer_idx] - ratios[:, layer_idx] * solved[layer_idx + 1]
    line_value = jnp.stack(solved, 1)
    centre = vel_pad[:, :, 1:-1, 1:-1]
    return ice_cover * ((1.0 - OMEGA) * centre + OMEGA * line_value)


def lane_weights(comps, width):
    along_x = jnp.concatenate(
        [jnp.full((width,), (4.0, 1.0)[c], jnp.float32) for c in range(comps)]
    )
    along_y = jnp.concatenate(
        [jnp.full((width,), (1.0, 4.0)[c], jnp.float32) for c in range(comps)]
    )
    return (along_x, along_y)


def prepare_lanes(visc_pad, beta_col, ice_cover, weights):
    faces = lateral_terms(visc_pad)
    west_face, east_face, south_face, north_face = faces
    along_x, along_y = weights
    centre_visc = visc_pad[:, 1:-1, 1:-1]
    vertical = VERTICAL * 0.5 * (centre_visc[:-1] + centre_visc[1:])
    zero_row = jnp.zeros_like(centre_visc[:1])
    upper_link = jnp.concatenate([vertical, zero_row], 0)
    lower_link = jnp.concatenate([zero_row, vertical], 0)
    basal = jnp.concatenate([jnp.zeros_like(centre_visc[:-1]), beta_col[None]], 0)
    diagonal = along_x * (west_face + east_face) + along_y * (south_face + north_face)
    diagonal = diagonal + upper_link + lower_link + basal + (1.0 - ice_cover)
    layer_count = visc_pad.shape[0]
    ratio_list = []
    inverse_list = []
    for layer_idx in range(layer_count):
        pivot = diagonal[layer_idx]
        if layer_idx > 0:
            pivot = pivot + lower_link[layer_idx] * ratio_list[-1]
        inverse = 1.0 / pivot
        inverse_list.append(inverse)
        ratio_list.append(-upper_link[layer_idx] * inverse)
    return (faces, lower_link, ratio_list, inverse_list)


def relax_lanes(vel_pad, rhs_field, faces, lower_link, ratios, inverses, ice_cover, weights):
    west_face, east_face, south_face, north_face = faces
    along_x, along_y = weights
    lateral = along_x * (west_face * vel_pad[:, :-2, 1:-1] + east_face * vel_pad[:, 2:, 1:-1])
    lateral = lateral + along_y * (
        south_face * vel_pad[:, 1:-1, :-2] + north_face * vel_pad[:, 1:-1, 2:]
    )
    right_side = rhs_field + lateral
    layer_count = right_side.shape[0]
    forward_list = []
    for layer_idx in range(layer_count):
        value = right_side[layer_idx]
        if layer_idx > 0:
            value = value + lower_link[layer_idx] * forward_list[-1]
        forward_list.append(value * inverses[layer_idx])
    solved = [None] * layer_count
    solved[layer_count - 1] = forward_list[layer_count - 1]
    for layer_idx in range(layer_count - 2, -1, -1):
        solved[layer_idx] = forward_list[layer_idx] - ratios[layer_idx] * solved[layer_idx + 1]
    line_value = jnp.stack(solved, 0)
    centre = vel_pad[:, 1:-1, 1:-1]
    return ice_cover * ((1.0 - OMEGA) * centre + OMEGA * line_value)


def pad_cells(field):
    return jnp.pad(field, [(0, 0)] * (field.ndim - 2) + [(1, 1), (1, 1)])


def shifted(piece, axis, down):
    count = lax.axis_size(axis)
    if down:
        pairs = [(i, i + 1) for i in range(count - 1)]
    else:
        pairs = [(i + 1, i) for i in range(count - 1)]
    return lax.ppermute(piece, axis, pairs)


def local(forcing, viscosity, observed, beta_tiles, ice_mask, tile_owner):
    comps, layers, rows, cols = forcing.shape
    tiles_here = beta_tiles.shape[1]
    float_planes = [forcing.reshape(comps * layers, rows, cols), viscosity, observed]
    int_planes = [ice_mask[None], tile_owner[None]]

    def pieces(rows_at, cols_at):
        return [p[:, rows_at, cols_at] for p in float_planes] + [
            p[:, rows_at, cols_at].astype(jnp.float32) for p in int_planes
        ]

    plane_count = sum((p.shape[0] for p in float_planes + int_planes))
    every = slice(None)
    beta_plane = jnp.pad(beta_tiles, ((0, HALO - 1), (0, cols - tiles_here)))[None]
    head = jnp.concatenate(pieces(slice(0, HALO), every) + [beta_plane], axis=0)
    tail = jnp.concatenate(pieces(slice(rows - HALO, rows), every) + [beta_plane], axis=0)
    from_above = shifted(tail, "gx", True)
    from_below = shifted(head, "gx", False)

    def stack_rows(lo, hi):
        return jnp.concatenate(
            [from_above[:plane_count, :, lo:hi]]
            + [jnp.concatenate(pieces(every, slice(lo, hi)), axis=0)]
            + [from_below[:plane_count, :, lo:hi]],
            axis=1,
        )

    from_left = shifted(stack_rows(cols - HALO, cols), "gy", True)
    from_right = shifted(stack_rows(0, HALO), "gy", False)
    strips_near = jnp.stack(
        [
            from_above[plane_count, 0, :tiles_here],
            beta_tiles[0],
            from_below[plane_count, 0, :tiles_here],
        ]
    )
    friction_rows = lax.all_gather(strips_near, "gy", axis=1, tiled=True)
    tile_count = friction_rows.shape[1]
    packed = jnp.concatenate([from_left, stack_rows(0, cols), from_right], axis=2)
    ext_rows, ext_cols = (packed.shape[1], packed.shape[2])
    at = 0
    forcing_ext = packed[at : at + comps * layers].reshape(comps, layers, ext_rows, ext_cols)
    at += comps * layers
    visc_ext = packed[at : at + layers]
    at += layers
    observed_ext = packed[at : at + comps]
    at += comps
    ice_cover = packed[at]
    owner_ext = packed[at + 1].astype(jnp.int32)
    tiles = lax.broadcasted_iota(jnp.int32, (tile_count, 1, 1), 0)
    owner_match = owner_ext[None] == tiles
    row_strip = jnp.concatenate(
        [
            jnp.broadcast_to(friction_rows[0][:, None], (tile_count, HALO)),
            jnp.broadcast_to(friction_rows[1][:, None], (tile_count, rows)),
            jnp.broadcast_to(friction_rows[2][:, None], (tile_count, HALO)),
        ],
        axis=1,
    )
    beta_col = jnp.sum(jnp.where(owner_match, row_strip[:, :, None], 0.0), axis=0)

    def side_by_side(per_comp):
        return jnp.concatenate([per_comp[c] for c in range(comps)], axis=-1)

    weights = lane_weights(comps, ext_cols)
    visc_lanes = side_by_side([visc_ext] * comps)
    ice_lanes = side_by_side([ice_cover] * comps)
    beta_lanes = side_by_side([beta_col] * comps)
    forcing_lanes = side_by_side([forcing_ext[c] for c in range(comps)])
    observed_lanes = side_by_side([observed_ext[c] for c in range(comps)])
    faces, lower_link, ratios, inverses = prepare_lanes(
        pad_cells(visc_lanes), beta_lanes, ice_lanes, weights
    )

    def advance(field, rhs_field):
        return relax_lanes(
            pad_cells(field), rhs_field, faces, lower_link, ratios, inverses, ice_lanes, weights
        )

    velocity = jnp.zeros_like(forcing_lanes)
    for sweep_idx in range(PASSES):
        velocity = advance(velocity, forcing_lanes)
    misfit = velocity[0] - observed_lanes
    adjoint_rhs = jnp.zeros_like(forcing_lanes).at[0].set(misfit)
    adjoint = jnp.zeros_like(forcing_lanes)
    for sweep_idx in range(PASSES):
        adjoint = advance(adjoint, adjoint_rhs)
    inner = (slice(HALO, HALO + rows), slice(HALO, HALO + cols))

    def split(field):
        return jnp.stack(
            [
                field[:, inner[0], c * ext_cols + HALO : c * ext_cols + HALO + cols]
                for c in range(comps)
            ]
        )

    velocity = split(velocity)
    adjoint = split(adjoint)
    grad_col = (
        -ice_cover[inner] * beta_col[inner] * jnp.sum(adjoint[:, -1] * velocity[:, -1], axis=0)
    )
    high = lax.reduce_precision(grad_col, exponent_bits=8, mantissa_bits=7)
    rest = grad_col - high
    middle = lax.reduce_precision(rest, exponent_bits=8, mantissa_bits=7)
    low = rest - middle
    parts = jnp.stack([high, middle, low], axis=-1).reshape(rows * cols, 3).astype(jnp.bfloat16)
    block_match = tile_owner.reshape(rows * cols, 1) == lax.broadcasted_iota(
        jnp.int32, (1, tile_count), 1
    )
    per_part = lax.dot_general(
        block_match.astype(jnp.bfloat16),
        parts,
        (((0,), (0,)), ((), ())),
        preferred_element_type=jnp.float32,
    )
    partial_sum = per_part[:, 0] + per_part[:, 1] + per_part[:, 2]
    owners = lax.axis_size("gy")
    chunk = tile_count // owners
    gathered = lax.all_gather(partial_sum.reshape(owners, chunk), "gy")
    mine = lax.dynamic_index_in_dim(gathered, lax.axis_index("gy"), axis=1, keepdims=False)
    grad_tiles = jnp.sum(mine, axis=0)[None]
    return (velocity, adjoint, grad_tiles)


def solution(mesh):
    in_specs = (
        P(None, None, "gx", "gy"),
        P(None, "gx", "gy"),
        P(None, "gx", "gy"),
        P("gx", "gy"),
        P("gx", "gy"),
        P("gx", "gy"),
    )
    out_specs = (P(None, None, "gx", "gy"), P(None, None, "gx", "gy"), P("gx", "gy"))
    return jax.shard_map(local, mesh=mesh, in_specs=in_specs, out_specs=out_specs, check_vma=False)
```

profile of v0, /device:TPU:0, one launch (start us, length us, event | category | flops | bytes accessed | tf_op | source)
XLA Modules:
  0.0 61.5 jit_solution(2362320991496488223)
XLA Ops:
  0.7 1.0 %constant_dynamic-update-slice_fusion.5 = (f32[53,7,128]{2,1,0:T(8,128)S(1)}, f32[53,7,128]{2,1,0:T(8,128)S(1)}) fusion(f32[32,16,128]{2,1,0:T(8,128)} %bitcast.64), kind=kLoop, calls=%fused_computation.47 | loop fusion | bytes 491520
  1.7 0.9 %constant_dynamic-update-slice_fusion.4 = (f32[53,7,128]{2,1,0:T(8,128)S(1)}, f32[53,7,128]{2,1,0:T(8,128)S(1)}) fusion(f32[53,7,128]{2,1,0:T(8,128)S(1)} %get-tuple-element.252, f32[16,16,128]{2,1,0:T(8,128)} %param.9, f32[53,7,128]{2,1,0:T(8,128)S(1)} %get-tuple-element.253), kind=kLoop, calls=%fused_computation.46 | loop fusion | bytes 245760
  2.6 0.7 %constant_dynamic-update-slice_fusion.3 = (f32[53,7,128]{2,1,0:T(8,128)S(1)}, f32[53,7,128]{2,1,0:T(8,128)S(1)}) fusion(f32[53,7,128]{2,1,0:T(8,128)S(1)} %get-tuple-element.260, f32[2,16,128]{2,1,0:T(8,128)} %param.10, f32[53,7,128]{2,1,0:T(8,128)S(1)} %get-tuple-element.261), kind=kLoop, calls=%fused_computation.45 | loop fusion | bytes 30720
  3.3 0.7 %constant_dynamic-update-slice_fusion.2 = (f32[53,7,128]{2,1,0:T(8,128)S(1)}, f32[53,7,128]{2,1,0:T(8,128)S(1)}) fusion(f32[53,7,128]{2,1,0:T(8,128)S(1)} %get-tuple-element.271, s32[1,16,128]{2,1,0:T(8,128)} %bitcast.67, f32[53,7,128]{2,1,0:T(8,128)S(1)} %get-tuple-element.272), kind=kLoop, calls=%fused_computation.44 | loop fusion | flops 1792 | bytes 15360
  4.1 0.7 %constant_dynamic-update-slice_fusion.1 = (f32[53,7,128]{2,1,0:T(8,128)S(1)}, f32[53,7,128]{2,1,0:T(8,128)S(1)}) fusion(f32[53,7,128]{2,1,0:T(8,128)S(1)} %get-tuple-element.281, s32[1,16,128]{2,1,0:T(8,128)} %bitcast.69, f32[53,7,128]{2,1,0:T(8,128)S(1)} %get-tuple-element.282), kind=kLoop, calls=%fused_computation.43 | loop fusion | flops 1792 | bytes 15360
  4.8 0.7 %constant_dynamic-update-slice_fusion = (f32[53,7,128]{2,1,0:T(8,128)S(1)}, f32[53,7,128]{2,1,0:T(8,128)S(1)}) fusion(f32[53,7,128]{2,1,0:T(8,128)S(1)} %get-tuple-element.279, f32[1,16]{1,0:T(1,128)} %param.11, f32[53,7,128]{2,1,0:T(8,128)S(1)} %get-tuple-element.280), kind=kLoop, calls=%fused_computation.42 | loop fusion | bytes 8256 | tf_op jit(solution)/shard_map/concatenate | solution.py:180
  5.4 1.3 %collective-permute-start.1 = (f32[53,7,128]{2,1,0:T(8,128)S(1)}, f32[53,7,128]{2,1,0:T(8,128)S(1)}, u32[]{:S(2)}, u32[]{:S(2)}) collective-permute-start(f32[53,7,128]{2,1,0:T(8,128)S(1)} %get-tuple-element.287), channel_id=1, source_target_pairs={{8,0},{16,8},{24,16},{9,1},{17,9},{25,17},{10,2},{18,10},{26,18},{... | collective-permute-start | bytes 569864 | tf_op jit(solution)/shard_map/ppermute | solution.py:162
  6.7 5.6 %collective-permute-start = (f32[53,7,128]{2,1,0:T(8,128)S(1)}, f32[53,7,128]{2,1,0:T(8,128)S(1)}, u32[]{:S(2)}, u32[]{:S(2)}) collective-permute-start(f32[53,7,128]{2,1,0:T(8,128)S(1)} %get-tuple-element.286), channel_id=1, source_target_pairs={{0,8},{8,16},{16,24},{1,9},{9,17},{17,25},{2,10},{10,18},{18,26},{... | collective-permute-start | bytes 569864 | tf_op jit(solution)/shard_map/ppermute | solution.py:162
  12.3 1.2 %fusion.298 = (f32[32,16,7]{2,1,0:T(8,128)S(1)}, f32[32,16,7]{2,1,0:T(8,128)S(1)}) fusion(f32[32,16,128]{2,1,0:T(8,128)} %bitcast.65), kind=kLoop, calls=%fused_computation.671 | loop fusion | bytes 57344 | tf_op jit(solution)/shard_map/slice | solution.py:172
  17.2 1.3 %collective-permute-start.3 = (f32[52,30,7]{0,1,2:T(8,128)S(1)}, f32[52,30,7]{0,1,2:T(8,128)S(1)}, u32[]{:S(2)}, u32[]{:S(2)}) collective-permute-start(f32[52,30,7]{0,1,2:T(8,128)S(1)} %pad_maximum_fusion.6), channel_id=1, source_target_pairs={{1,0},{2,1},{3,2},{4,3},{5,4},{6,5},{7,6},{9,8},{10,9},{11,10},{12... | collective-permute-start | bytes 131048 | tf_op jit(solution)/shard_map/ppermute | solution.py:162
  18.8 3.0 %collective-permute-start.2 = (f32[52,30,7]{0,1,2:T(8,128)S(1)}, f32[52,30,7]{0,1,2:T(8,128)S(1)}, u32[]{:S(2)}, u32[]{:S(2)}) collective-permute-start(f32[52,30,7]{0,1,2:T(8,128)S(1)} %pad_maximum_fusion.5), channel_id=1, source_target_pairs={{0,1},{1,2},{2,3},{3,4},{4,5},{5,6},{6,7},{8,9},{9,10},{10,11},{11... | collective-permute-start | bytes 131048 | tf_op jit(solution)/shard_map/ppermute | solution.py:162
  21.9 9.2 %all-gather = f32[8,16,3]{1,2,0:T(4,128)S(1)} all-gather(f32[1,16,3]{1,2,0:T(4,128)S(1)} %maximum_bitcast_fusion.2), channel_id=1, replica_groups=mesh['gx'=4,'gy'=8] {'gy'}, dimensions={0}, use_global_device_ids=true | all-gather | bytes 1728 | tf_op jit(solution)/shard_map/all_gather | solution.py:201
  31.3 0.8 %copy.65 = f32[52,30,7]{2,1,0:T(8,128)S(1)} copy(f32[52,30,7]{0,1,2:T(8,128)S(1)} %collective-permute-done.3) | data formatting | bytes 87360 | tf_op jit(solution)/shard_map/ppermute | solution.py:162
  32.2 0.9 %copy.64 = f32[52,30,7]{2,1,0:T(8,128)S(1)} copy(f32[52,30,7]{0,1,2:T(8,128)S(1)} %collective-permute-done.2) | data formatting | bytes 87360 | tf_op jit(solution)/shard_map/ppermute | solution.py:162
  33.0 1.0 %pad_maximum_fusion = f32[52,30,142]{2,1,0:T(8,128)S(1)} fusion(f32[52,30,7]{2,1,0:T(8,128)S(1)} %copy.65, f32[52,7,128]{2,1,0:T(8,128)S(1)} %slice.1159, f32[52,16,128]{2,1,0:T(8,128)S(1)} %constant_dynamic-update-slice_fusion.12, f32[52,7,128]{2,1,0:T(8,128)S(1)} %slice.1158, f32[52,30,7]{2,1,0:T(8,128)S(1)} %copy.64), kind=kLoop, calls=%fused_computation.2 | loop fusion | flops 886080 | bytes 1772160 | tf_op jit(solution)/shard_map/concatenate | solution.py:203
  34.3 0.3 fusion.3
  34.8 2.2 %select_reduce_fusion = f32[30,142]{1,0:T(8,128)S(1)} fusion(f32[128,30]{0,1:T(8,128)S(1)} %pad_maximum_fusion.16, s32[30,142]{1,0:T(8,128)S(1)} %get-tuple-element.242), kind=kLoop, calls=%fused_computation | loop fusion | flops 1631580 | bytes 49440 | tf_op jit(solution)/shard_map/reduce_sum | solution.py:224
  37.2 0.8 %fusion.167 = (f32[16,30,284]{2,1,0:T(8,128)S(1)}, f32[16,30,284]{2,1,0:T(8,128)S(1)}, f32[16,30,284]{2,1,0:T(8,128)S(1)}, f32[16,30,284]{2,1,0:T(8,128)S(1)}, f...) fusion(f32[16,30,142]{2,1,0:T(8,128)S(1)} %get-tuple-element.244, f32[16,30,142]{2,1,0:T(8,128)S(1)} %get-tuple-element.245, ...), kind=kLoop, calls=%fused_computation.669 | loop fusion | flops 2044800 | bytes 4500832 | tf_op jit(solution)/shard_map/add | solution.py:135
  38.0 0.4 add_add_fusion.3
  38.5 0.3 fusion.126
  39.3 0.9 %add_add_fusion.2 = f32[16,30,284]{2,1,0:T(8,128)S(1)} fusion(f32[16,30,284]{2,1,0:T(8,128)S(1)} %broadcast_multiply_fusion.1, f32[16,30,284]{2,1,0:T(8,128)S(1)} %get-tuple-element.240, f32[16,30,284]{2,1,0:T(8,128)S(1)} %get-tuple-element.239, f32[16,30,284]{2,1,0:T(8,128)S(1)} %get-tuple-element.238, f32[16,30,284]{2,1,0:T(8,128)S(1)} %get-tuple-element.237, ...), kind=kLoop, calls=%fused_computation.22 | loop fusion | flops 2044800 | bytes 3819232 | tf_op jit(solution)/shard_map/add | solution.py:135
  40.9 0.9 %add_add_fusion.1 = f32[16,30,284]{2,1,0:T(8,128)S(1)} fusion(f32[16,30,284]{2,1,0:T(8,128)S(1)} %add_multiply_fusion.5, f32[16,30,284]{2,1,0:T(8,128)S(1)} %get-tuple-element.240, f32[16,30,284]{2,1,0:T(8,128)S(1)} %get-tuple-element.239, f32[16,30,284]{2,1,0:T(8,128)S(1)} %get-tuple-element.238, f32[16,30,284]{2,1,0:T(8,128)S(1)} %get-tuple-element.237, ...), kind=kLoop, calls=%fused_computation.20 | loop fusion | flops 2044800 | bytes 3819232 | tf_op jit(solution)/shard_map/add | solution.py:135
  42.6 0.9 %add_add_fusion = f32[16,30,284]{2,1,0:T(8,128)S(1)} fusion(f32[16,30,284]{2,1,0:T(8,128)S(1)} %add_multiply_fusion.4, f32[16,30,284]{2,1,0:T(8,128)S(1)} %get-tuple-element.240, f32[16,30,284]{2,1,0:T(8,128)S(1)} %get-tuple-element.239, f32[16,30,284]{2,1,0:T(8,128)S(1)} %get-tuple-element.238, f32[16,30,284]{2,1,0:T(8,128)S(1)} %get-tuple-element.237, ...), kind=kLoop, calls=%fused_computation.18 | loop fusion | flops 2044800 | bytes 3819232 | tf_op jit(solution)/shard_map/add | solution.py:135
  44.2 0.2 fusion.60
  44.9 0.8 %multiply_add_fusion.2 = f32[16,30,284]{2,1,0:T(8,128)S(1)} fusion(f32[16,30,284]{2,1,0:T(8,128)S(1)} %broadcast_multiply_fusion, f32[16,30,284]{2,1,0:T(8,128)S(1)} %get-tuple-element.240, f32[16,30,284]{2,1,0:T(8,128)S(1)} %get-tuple-element.239, f32[16,30,284]{2,1,0:T(8,128)S(1)} %get-tuple-element.238, f32[16,30,284]{2,1,0:T(8,128)S(1)} %get-tuple-element.237, ...), kind=kLoop, calls=%fused_computation.16 | loop fusion | flops 1772160 | bytes 3273952 | tf_op jit(solution)/shard_map/add | solution.py:132
  46.5 0.8 %multiply_add_fusion.1 = f32[16,30,284]{2,1,0:T(8,128)S(1)} fusion(f32[16,30,284]{2,1,0:T(8,128)S(1)} %add_multiply_fusion.2, f32[16,30,284]{2,1,0:T(8,128)S(1)} %get-tuple-element.240, f32[16,30,284]{2,1,0:T(8,128)S(1)} %get-tuple-element.239, f32[16,30,284]{2,1,0:T(8,128)S(1)} %get-tuple-element.238, f32[16,30,284]{2,1,0:T(8,128)S(1)} %get-tuple-element.237, ...), kind=kLoop, calls=%fused_computation.14 | loop fusion | flops 1772160 | bytes 3273952 | tf_op jit(solution)/shard_map/add | solution.py:132
  48.0 0.8 %multiply_add_fusion = f32[16,30,284]{2,1,0:T(8,128)S(1)} fusion(f32[16,30,284]{2,1,0:T(8,128)S(1)} %add_multiply_fusion.1, f32[16,30,284]{2,1,0:T(8,128)S(1)} %get-tuple-element.240, f32[16,30,284]{2,1,0:T(8,128)S(1)} %get-tuple-element.239, f32[16,30,284]{2,1,0:T(8,128)S(1)} %get-tuple-element.238, f32[16,30,284]{2,1,0:T(8,128)S(1)} %get-tuple-element.237, ...), kind=kLoop, calls=%fused_computation.12 | loop fusion | flops 1772160 | bytes 3273952 | tf_op jit(solution)/shard_map/add | solution.py:132
  49.8 0.7 %pad_maximum_fusion.3 = f32[2,16,16,128]{3,2,1,0:T(8,128)} fusion(f32[1,16,16,128]{3,2,1,0:T(8,128)S(1)} %get-tuple-element.288, f32[1,16,16,128]{3,2,1,0:T(8,128)S(1)} %get-tuple-element.289), kind=kLoop, calls=%fused_computation.37 | loop fusion | flops 65536 | bytes 524288 | tf_op jit(solution)/shard_map/stack | solution.py:255
  50.5 0.7 %pad_maximum_fusion.4 = f32[2,16,16,128]{3,2,1,0:T(8,128)} fusion(f32[1,16,16,128]{3,2,1,0:T(8,128)S(1)} %get-tuple-element.247, f32[1,16,16,128]{3,2,1,0:T(8,128)S(1)} %get-tuple-element.246), kind=kLoop, calls=%fused_computation.40 | loop fusion | flops 65536 | bytes 524288 | tf_op jit(solution)/shard_map/stack | solution.py:255
  51.4 0.5 fusion
  51.9 9.1 %all_gather.7 = f32[8,8,16]{2,1,0:T(8,128)S(1)} all-gather(f32[1,8,16]{2,1,0:T(8,128)S(1)} %add.4639), channel_id=1, replica_groups=mesh['gx'=4,'gy'=8] {'gy'}, dimensions={0}, use_global_device_ids=true | all-gather | bytes 4608 | tf_op jit(solution)/shard_map/all_gather | solution.py:284
  61.0 0.5 dynamic-slice_reduce_fusion
  (219 shorter events, 9.6 us)
Async XLA Ops:
  0.6 13.2 %copy-start = (f32[2,16,16,128]{3,2,1,0:T(8,128)S(1)}, f32[2,16,16,128]{3,2,1,0:T(8,128)}, u32[]{:S(2)}) copy-start(f32[2,16,16,128]{3,2,1,0:T(8,128)} %param.8) | copy-start | bytes 786436
  0.6 12.8 %copy-start.1 = (f32[16,16,128]{2,1,0:T(8,128)S(1)}, f32[16,16,128]{2,1,0:T(8,128)}, u32[]{:S(2)}) copy-start(f32[16,16,128]{2,1,0:T(8,128)} %param.9) | copy-start | bytes 393220
  0.7 12.9 %copy-start.2 = (f32[2,16,128]{2,1,0:T(8,128)S(1)}, f32[2,16,128]{2,1,0:T(8,128)}, u32[]{:S(2)}) copy-start(f32[2,16,128]{2,1,0:T(8,128)} %param.10) | copy-start | bytes 49156
  0.7 13.0 %copy-start.5 = (s32[16,128]{1,0:T(8,128)S(1)}, s32[16,128]{1,0:T(8,128)}, u32[]{:S(2)}) copy-start(s32[16,128]{1,0:T(8,128)} %param.12) | copy-start | bytes 24580
  0.7 13.0 %copy-start.6 = (s32[16,128]{1,0:T(8,128)S(1)}, s32[16,128]{1,0:T(8,128)}, u32[]{:S(2)}) copy-start(s32[16,128]{1,0:T(8,128)} %param.13) | copy-start | bytes 24580
  5.4 11.0 %collective-permute-start.1 = (f32[53,7,128]{2,1,0:T(8,128)S(1)}, f32[53,7,128]{2,1,0:T(8,128)S(1)}, u32[]{:S(2)}, u32[]{:S(2)}) collective-permute-start(f32[53,7,128]{2,1,0:T(8,128)S(1)} %get-tuple-element.287), channel_id=1, source_target_pairs={{8,0},{16,8},{24,16},{9,1},{17,9},{25,17},{10,2},{18,10},{26,18},{... | collective-permute-start | bytes 569864 | tf_op jit(solution)/shard_map/ppermute | solution.py:162
  6.7 10.1 %collective-permute-start = (f32[53,7,128]{2,1,0:T(8,128)S(1)}, f32[53,7,128]{2,1,0:T(8,128)S(1)}, u32[]{:S(2)}, u32[]{:S(2)}) collective-permute-start(f32[53,7,128]{2,1,0:T(8,128)S(1)} %get-tuple-element.286), channel_id=1, source_target_pairs={{0,8},{8,16},{16,24},{1,9},{9,17},{17,25},{2,10},{10,18},{18,26},{... | collective-permute-start | bytes 569864 | tf_op jit(solution)/shard_map/ppermute | solution.py:162
  16.2 5.7 %copy-start.7 = (f32[1,16]{1,0:T(1,128)S(1)}, f32[1,16]{1,0:T(1,128)}, u32[]{:S(2)}) copy-start(f32[1,16]{1,0:T(1,128)} %param.11) | copy-start | bytes 196
  17.2 14.1 %collective-permute-start.3 = (f32[52,30,7]{0,1,2:T(8,128)S(1)}, f32[52,30,7]{0,1,2:T(8,128)S(1)}, u32[]{:S(2)}, u32[]{:S(2)}) collective-permute-start(f32[52,30,7]{0,1,2:T(8,128)S(1)} %pad_maximum_fusion.6), channel_id=1, source_target_pairs={{1,0},{2,1},{3,2},{4,3},{5,4},{6,5},{7,6},{9,8},{10,9},{11,10},{12... | collective-permute-start | bytes 131048 | tf_op jit(solution)/shard_map/ppermute | solution.py:162
  18.8 13.3 %collective-permute-start.2 = (f32[52,30,7]{0,1,2:T(8,128)S(1)}, f32[52,30,7]{0,1,2:T(8,128)S(1)}, u32[]{:S(2)}, u32[]{:S(2)}) collective-permute-start(f32[52,30,7]{0,1,2:T(8,128)S(1)} %pad_maximum_fusion.5), channel_id=1, source_target_pairs={{0,1},{1,2},{2,3},{3,4},{4,5},{5,6},{6,7},{8,9},{9,10},{10,11},{11... | collective-permute-start | bytes 131048 | tf_op jit(solution)/shard_map/ppermute | solution.py:162
  34.7 2.5 %copy-start.3 = (f32[284]{0:T(512)S(1)}, f32[284]{0:T(512)}, u32[]{:S(2)}) copy-start(f32[284]{0:T(512)} %constant.51.clone.1) | copy-start | bytes 3412
  34.7 2.5 %copy-start.4 = (f32[284]{0:T(512)S(1)}, f32[284]{0:T(512)}, u32[]{:S(2)}) copy-start(f32[284]{0:T(512)} %constant.49.clone.1) | copy-start | bytes 3412
where the time goes:
time: 62 us; the launch traced here: 61.5 us
  other arithmetic  18.8 us (30%)
  blocking collectives  18.3 us (30%)
  starting transfers between devices  11.2 us (18%)
  local copies, waits for them, and re-layouts  10.6 us (17%)
  between operations  2.09 us (3%)
    ppermute x4, starting transfers between devices, shifted(): return lax.ppermute(piece, axis, pairs)  11.2 us
    all_gather x1, blocking collectives, local(): friction_rows = lax.all_gather(strips_near, 'gy', axis=1, tiled=True)  9.2 us
    all_gather x1, blocking collectives, local(): gathered = lax.all_gather(partial_sum.reshape(owners, chunk), 'gy')  9.05 us
    unnamed x86, local copies, waits for them, and re-layouts  4.03 us
    add x4, other arithmetic, relax_lanes(): right_side = rhs_field + lateral  3.52 us
    unnamed x70, other arithmetic  3.46 us
    add x3, other arithmetic, relax_lanes(): lateral + along_y * (south_face * vel_pad[:, 1:-1, :-2] + north_face * ve...  2.35 us
    reduce_sum x1, other arithmetic, local(): jnp.sum(jnp.where(owner_match, row_strip[:, :, None], 0.0), axis=0)  2.23 us
  transfers between devices with their start and end apart: 4, of which 1 were waited for; matrix products, arithmetic and copies ran while one was open for 9% of the time, Pallas kernels for 0%

commit v1 on v0

--- a/solution.py
+++ b/solution.py
@@ -7,6 +7,22 @@
 OMEGA = 0.8
 VERTICAL = 16.0
 HALO = 2 * PASSES - 1
+
+
+def gather_around(x, axis, dim):
+    ways, here, step = (lax.axis_size(axis), lax.axis_index(axis), x.shape[dim])
+    shape = [n * ways if d == dim else n for d, n in enumerate(x.shape)]
+    full = lax.dynamic_update_slice_in_dim(jnp.zeros(shape, x.dtype), x, here * step, axis=dim)
+    going_up = going_down = x
+    for far in range(1, ways // 2 + 1):
+        going_up = lax.ppermute(going_up, axis, [(d, (d + 1) % ways) for d in range(ways)])
+        full = lax.dynamic_update_slice_in_dim(full, going_up, (here - far) % ways * step, axis=dim)
+        if 2 * far < ways:
+            going_down = lax.ppermute(going_down, axis, [(d, (d - 1) % ways) for d in range(ways)])
+            full = lax.dynamic_update_slice_in_dim(
+                full, going_down, (here + far) % ways * step, axis=dim
+            )
+    return full
 
 
 def with_halo(cells, sides, width):
@@ -198,7 +214,7 @@
             from_below[plane_count, 0, :tiles_here],
         ]
     )
-    friction_rows = lax.all_gather(strips_near, "gy", axis=1, tiled=True)
+    friction_rows = gather_around(strips_near, "gy", 1)
     tile_count = friction_rows.shape[1]
     packed = jnp.concatenate([from_left, stack_rows(0, cols), from_right], axis=2)
     ext_rows, ext_cols = (packed.shape[1], packed.shape[2])

time: 62 us -> 70.6 us (1.14)
  blocking collectives: 18.3 us -> 11 us
  starting transfers between devices: 11.2 us -> 17.1 us
  waiting for transfers between devices: 0.18 us -> 5.98 us
  local copies, waits for them, and re-layouts: 10.6 us -> 12.9 us
  other arithmetic: 18.8 us -> 20.3 us
    all_gather x1 -> x0, blocking collectives: 9.2 us -> none  [local(): friction_rows = lax.all_gather(strips_near, 'gy', axis=1, tiled=True)]
    ppermute x0 -> x7, starting transfers between devices: none -> 6.24 us  [the longest x3 4.35 us: gather_around(): lax.ppermute(going_down, axis, [(d, (d - 1) % ways) for d in range(ways)])]
    ppermute x0 -> x7, waiting for transfers between devices: none -> 5.22 us  [the longest x4 5.17 us: gather_around(): lax.ppermute(going_up, axis, [(d, (d + 1) % ways) for d in range(ways)])]
    all_gather x1, blocking collectives: 9.05 us -> 11 us  [local(): gathered = lax.all_gather(partial_sum.reshape(owners, chunk), 'gy')]
    dynamic_update_slice x0 -> x8, local copies, waits for them, and re-layouts: none -> 1.59 us  [the longest x4 0.75 us: gather_around(): lax.dynamic_update_slice_in_dim(full, going_up, (here - far) % ways * ste...]
    convert_element_type x2, other arithmetic: 0.15 us -> 1.69 us  [pieces(): p[:, rows_at, cols_at].astype(jnp.float32)]
    slice x5, local copies, waits for them, and re-layouts: 1.71 us -> 2.47 us  [pieces(): p[:, rows_at, cols_at]]
    unnamed x86 -> x85, local copies, waits for them, and re-layouts: 4.03 us -> 3.93 us
  transfers between devices with their start and end apart: 4 -> 11, of which waited for: 1 -> 4; matrix products, arithmetic and copies ran while one was open for 9% -> 14% of each run, Pallas kernels for 0% -> 0%
where the time goes in v1:
time: 70.6 us; the launch traced here: 69.9 us
  other arithmetic  20.3 us (29%)
  starting transfers between devices  17.1 us (24%)
  local copies, waits for them, and re-layouts  12.9 us (18%)
  blocking collectives  11 us (16%)
  waiting for transfers between devices  5.98 us (8%)
  between operations  2.27 us (3%)
    all_gather x1, blocking collectives, local(): gathered = lax.all_gather(partial_sum.reshape(owners, chunk), 'gy')  11 us
    ppermute x4, starting transfers between devices, shifted(): return lax.ppermute(piece, axis, pairs)  10.8 us
    ppermute x4, waiting for transfers between devices, gather_around(): lax.ppermute(going_up, axis, [(d, (d + 1) % ways) for d in range(ways)])  5.17 us
    ppermute x3, starting transfers between devices, gather_around(): lax.ppermute(going_down, axis, [(d, (d - 1) % ways) for d in range(ways)])  4.35 us
    unnamed x85, local copies, waits for them, and re-layouts  3.93 us
    add x4, other arithmetic, relax_lanes(): right_side = rhs_field + lateral  3.52 us
    unnamed x69, other arithmetic  3.45 us
    slice x5, local copies, waits for them, and re-layouts, pieces(): p[:, rows_at, cols_at]  2.47 us
  transfers between devices with their start and end apart: 11, of which 4 were waited for; matrix products, arithmetic and copies ran while one was open for 14% of the time, Pallas kernels for 0%

profile of v1, /device:TPU:0, one launch (start us, length us, event | category | flops | bytes accessed | tf_op | source)
XLA Modules:
  0.0 69.9 jit_solution(16987477889107131573)
XLA Ops:
  0.6 1.0 %constant_dynamic-update-slice_fusion.5 = (f32[53,7,128]{2,1,0:T(8,128)S(1)}, f32[53,7,128]{2,1,0:T(8,128)S(1)}) fusion(f32[32,16,128]{2,1,0:T(8,128)} %bitcast.57), kind=kLoop, calls=%fused_computation.47 | loop fusion | bytes 491520
  1.7 0.9 %constant_dynamic-update-slice_fusion.4 = (f32[53,7,128]{2,1,0:T(8,128)S(1)}, f32[53,7,128]{2,1,0:T(8,128)S(1)}) fusion(f32[53,7,128]{2,1,0:T(8,128)S(1)} %get-tuple-element.252, f32[16,16,128]{2,1,0:T(8,128)} %param.9, f32[53,7,128]{2,1,0:T(8,128)S(1)} %get-tuple-element.253), kind=kLoop, calls=%fused_computation.46 | loop fusion | bytes 245760
  2.6 0.7 %constant_dynamic-update-slice_fusion.3 = (f32[53,7,128]{2,1,0:T(8,128)S(1)}, f32[53,7,128]{2,1,0:T(8,128)S(1)}) fusion(f32[53,7,128]{2,1,0:T(8,128)S(1)} %get-tuple-element.260, f32[2,16,128]{2,1,0:T(8,128)} %param.10, f32[53,7,128]{2,1,0:T(8,128)S(1)} %get-tuple-element.261), kind=kLoop, calls=%fused_computation.45 | loop fusion | bytes 30720
  5.4 4.9 %collective-permute-start = (f32[53,7,128]{2,1,0:T(8,128)S(1)}, f32[53,7,128]{2,1,0:T(8,128)S(1)}, u32[]{:S(2)}, u32[]{:S(2)}) collective-permute-start(f32[53,7,128]{2,1,0:T(8,128)S(1)} %get-tuple-element.286), channel_id=1, source_target_pairs={{0,8},{8,16},{16,24},{1,9},{9,17},{17,25},{2,10},{10,18},{18,26},{... | collective-permute-start | bytes 569864 | tf_op jit(solution)/shard_map/ppermute | solution.py:178
  10.3 1.3 %collective-permute-start.1 = (f32[53,7,128]{2,1,0:T(8,128)S(1)}, f32[53,7,128]{2,1,0:T(8,128)S(1)}, u32[]{:S(2)}, u32[]{:S(2)}) collective-permute-start(f32[53,7,128]{2,1,0:T(8,128)S(1)} %get-tuple-element.287), channel_id=1, source_target_pairs={{8,0},{16,8},{24,16},{9,1},{17,9},{25,17},{10,2},{18,10},{26,18},{... | collective-permute-start | bytes 569864 | tf_op jit(solution)/shard_map/ppermute | solution.py:178
  11.7 0.8 %slice_convert_fusion.3 = (f32[1,16,7]{2,1,0:T(8,128)S(1)}, f32[1,16,7]{2,1,0:T(8,128)S(1)}) fusion(s32[1,16,128]{2,1,0:T(8,128)} %bitcast.61), kind=kLoop, calls=%fused_computation.652 | loop fusion | flops 224 | bytes 1792 | tf_op jit(solution)/shard_map/convert_element_type | solution.py:189
  12.6 0.8 %slice_convert_fusion.2 = (f32[1,16,7]{2,1,0:T(8,128)S(1)}, f32[1,16,7]{2,1,0:T(8,128)S(1)}) fusion(s32[1,16,128]{2,1,0:T(8,128)} %bitcast.63), kind=kLoop, calls=%fused_computation.651 | loop fusion | flops 224 | bytes 1792 | tf_op jit(solution)/shard_map/convert_element_type | solution.py:189
  13.4 0.9 %fusion.302 = (f32[2,16,7]{2,1,0:T(8,128)S(1)}, f32[2,16,7]{2,1,0:T(8,128)S(1)}) fusion(f32[2,16,128]{2,1,0:T(8,128)} %param.10), kind=kLoop, calls=%fused_computation.675 | loop fusion | bytes 3584 | tf_op jit(solution)/shard_map/slice | solution.py:188
  14.3 1.1 %fusion.301 = (f32[16,16,7]{2,1,0:T(8,128)S(1)}, f32[16,16,7]{2,1,0:T(8,128)S(1)}) fusion(f32[16,16,128]{2,1,0:T(8,128)} %param.9), kind=kLoop, calls=%fused_computation.674 | loop fusion | bytes 28672 | tf_op jit(solution)/shard_map/slice | solution.py:188
  18.2 0.8 %collective-permute-done.1 = f32[53,7,128]{2,1,0:T(8,128)S(1)} collective-permute-done((f32[53,7,128]{2,1,0:T(8,128)S(1)}, f32[53,7,128]{2,1,0:T(8,128)S(1)}, u32[]{:S(2)}, u32[]{:S(2)}) %collective-permute-start.1) | collective-permute-done | bytes 189984 | tf_op jit(solution)/shard_map/ppermute | solution.py:178
  19.0 0.9 %collective-permute-start.5 = (f32[3,16]{1,0:T(4,128)S(1)}, f32[3,16]{1,0:T(4,128)S(1)}, u32[]{:S(2)}, u32[]{:S(2)}) collective-permute-start(f32[3,16]{1,0:T(4,128)S(1)} %pad_maximum_fusion.17), channel_id=1, source_target_pairs={{0,7},{1,0},{2,1},{3,2},{4,3},{5,4},{6,5},{7,6},{8,15},{9,8},{10,9... | collective-permute-start | bytes 584 | tf_op jit(solution)/shard_map/ppermute | solution.py:21
  20.9 1.3 %collective-permute-start.3 = (f32[52,30,7]{0,1,2:T(8,128)S(1)}, f32[52,30,7]{0,1,2:T(8,128)S(1)}, u32[]{:S(2)}, u32[]{:S(2)}) collective-permute-start(f32[52,30,7]{0,1,2:T(8,128)S(1)} %pad_maximum_fusion.6), channel_id=1, source_target_pairs={{1,0},{2,1},{3,2},{4,3},{5,4},{6,5},{7,6},{9,8},{10,9},{11,10},{12... | collective-permute-start | bytes 131048 | tf_op jit(solution)/shard_map/ppermute | solution.py:178
  22.2 3.3 %collective-permute-start.2 = (f32[52,30,7]{0,1,2:T(8,128)S(1)}, f32[52,30,7]{0,1,2:T(8,128)S(1)}, u32[]{:S(2)}, u32[]{:S(2)}) collective-permute-start(f32[52,30,7]{0,1,2:T(8,128)S(1)} %pad_maximum_fusion.5), channel_id=1, source_target_pairs={{0,1},{1,2},{2,3},{3,4},{4,5},{5,6},{6,7},{8,9},{9,10},{10,11},{11... | collective-permute-start | bytes 131048 | tf_op jit(solution)/shard_map/ppermute | solution.py:178
  25.8 1.9 %collective-permute-start.6 = (f32[3,16]{1,0:T(4,128)S(1)}, f32[3,16]{1,0:T(4,128)S(1)}, u32[]{:S(2)}, u32[]{:S(2)}) collective-permute-start(f32[3,16]{1,0:T(4,128)S(1)} %collective-permute-done.4), channel_id=1, source_target_pairs={{0,1},{1,2},{2,3},{3,4},{4,5},{5,6},{6,7},{7,0},{8,9},{9,10},{10,1... | collective-permute-start | bytes 584 | tf_op jit(solution)/shard_map/ppermute | solution.py:18
  27.7 0.8 %collective-permute-start.7 = (f32[3,16]{1,0:T(4,128)S(1)}, f32[3,16]{1,0:T(4,128)S(1)}, u32[]{:S(2)}, u32[]{:S(2)}) collective-permute-start(f32[3,16]{1,0:T(4,128)S(1)} %collective-permute-done.5), channel_id=1, source_target_pairs={{0,7},{1,0},{2,1},{3,2},{4,3},{5,4},{6,5},{7,6},{8,15},{9,8},{10,9... | collective-permute-start | bytes 584 | tf_op jit(solution)/shard_map/ppermute | solution.py:21
  28.9 0.9 %collective-permute-done.6 = f32[3,16]{1,0:T(4,128)S(1)} collective-permute-done((f32[3,16]{1,0:T(4,128)S(1)}, f32[3,16]{1,0:T(4,128)S(1)}, u32[]{:S(2)}, u32[]{:S(2)}) %collective-permute-start.6) | collective-permute-done | bytes 224 | tf_op jit(solution)/shard_map/ppermute | solution.py:18
  29.8 2.6 %collective-permute-start.9 = (f32[3,16]{1,0:T(4,128)S(1)}, f32[3,16]{1,0:T(4,128)S(1)}, u32[]{:S(2)}, u32[]{:S(2)}) collective-permute-start(f32[3,16]{1,0:T(4,128)S(1)} %collective-permute-done.7), channel_id=1, source_target_pairs={{0,7},{1,0},{2,1},{3,2},{4,3},{5,4},{6,5},{7,6},{8,15},{9,8},{10,9... | collective-permute-start | bytes 584 | tf_op jit(solution)/shard_map/ppermute | solution.py:21
  32.8 0.9 %collective-permute-done.8 = f32[3,16]{1,0:T(4,128)S(1)} collective-permute-done((f32[3,16]{1,0:T(4,128)S(1)}, f32[3,16]{1,0:T(4,128)S(1)}, u32[]{:S(2)}, u32[]{:S(2)}) %collective-permute-start.8) | collective-permute-done | bytes 224 | tf_op jit(solution)/shard_map/ppermute | solution.py:18
  34.1 3.5 %collective-permute-done.10 = f32[3,16]{1,0:T(4,128)S(1)} collective-permute-done((f32[3,16]{1,0:T(4,128)S(1)}, f32[3,16]{1,0:T(4,128)S(1)}, u32[]{:S(2)}, u32[]{:S(2)}) %collective-permute-start.10) | collective-permute-done | bytes 224 | tf_op jit(solution)/shard_map/ppermute | solution.py:18
  37.8 0.8 %copy.61 = f32[52,30,7]{2,1,0:T(8,128)S(1)} copy(f32[52,30,7]{0,1,2:T(8,128)S(1)} %collective-permute-done.2) | data formatting | bytes 87360 | tf_op jit(solution)/shard_map/ppermute | solution.py:178
  38.7 0.9 %copy.62 = f32[52,30,7]{2,1,0:T(8,128)S(1)} copy(f32[52,30,7]{0,1,2:T(8,128)S(1)} %collective-permute-done.3) | data formatting | bytes 87360 | tf_op jit(solution)/shard_map/ppermute | solution.py:178
  39.6 1.0 %pad_maximum_fusion = f32[52,30,142]{2,1,0:T(8,128)S(1)} fusion(f32[52,30,7]{2,1,0:T(8,128)S(1)} %copy.62, f32[52,7,128]{2,1,0:T(8,128)S(1)} %slice.1159, f32[52,16,128]{2,1,0:T(8,128)S(1)} %constant_dynamic-update-slice_fusion.12, f32[52,7,128]{2,1,0:T(8,128)S(1)} %slice.1158, f32[52,30,7]{2,1,0:T(8,128)S(1)} %copy.61), kind=kLoop, calls=%fused_computation.2 | loop fusion | flops 886080 | bytes 1772160 | tf_op jit(solution)/shard_map/concatenate | solution.py:219
  41.3 2.2 %select_reduce_fusion = f32[30,142]{1,0:T(8,128)S(1)} fusion(f32[128,30]{0,1:T(8,128)S(1)} %pad_maximum_fusion.16, s32[30,142]{1,0:T(8,128)S(1)} %get-tuple-element.242), kind=kLoop, calls=%fused_computation | loop fusion | flops 1631580 | bytes 49440 | tf_op jit(solution)/shard_map/reduce_sum | solution.py:240
  43.7 0.8 %fusion.167 = (f32[16,30,284]{2,1,0:T(8,128)S(1)}, f32[16,30,284]{2,1,0:T(8,128)S(1)}, f32[16,30,284]{2,1,0:T(8,128)S(1)}, f32[16,30,284]{2,1,0:T(8,128)S(1)}, f...) fusion(f32[16,30,142]{2,1,0:T(8,128)S(1)} %get-tuple-element.244, f32[16,30,142]{2,1,0:T(8,128)S(1)} %get-tuple-element.245, ...), kind=kLoop, calls=%fused_computation.669 | loop fusion | flops 2044800 | bytes 4500832 | tf_op jit(solution)/shard_map/add | solution.py:151
  45.7 0.9 %add_add_fusion.2 = f32[16,30,284]{2,1,0:T(8,128)S(1)} fusion(f32[16,30,284]{2,1,0:T(8,128)S(1)} %broadcast_multiply_fusion.1, f32[16,30,284]{2,1,0:T(8,128)S(1)} %get-tuple-element.240, f32[16,30,284]{2,1,0:T(8,128)S(1)} %get-tuple-element.239, f32[16,30,284]{2,1,0:T(8,128)S(1)} %get-tuple-element.238, f32[16,30,284]{2,1,0:T(8,128)S(1)} %get-tuple-element.237, ...), kind=kLoop, calls=%fused_computation.22 | loop fusion | flops 2044800 | bytes 3819232 | tf_op jit(solution)/shard_map/add | solution.py:151
  47.4 0.9 %add_add_fusion.1 = f32[16,30,284]{2,1,0:T(8,128)S(1)} fusion(f32[16,30,284]{2,1,0:T(8,128)S(1)} %add_multiply_fusion.5, f32[16,30,284]{2,1,0:T(8,128)S(1)} %get-tuple-element.240, f32[16,30,284]{2,1,0:T(8,128)S(1)} %get-tuple-element.239, f32[16,30,284]{2,1,0:T(8,128)S(1)} %get-tuple-element.238, f32[16,30,284]{2,1,0:T(8,128)S(1)} %get-tuple-element.237, ...), kind=kLoop, calls=%fused_computation.20 | loop fusion | flops 2044800 | bytes 3819232 | tf_op jit(solution)/shard_map/add | solution.py:151
  49.0 0.9 %add_add_fusion = f32[16,30,284]{2,1,0:T(8,128)S(1)} fusion(f32[16,30,284]{2,1,0:T(8,128)S(1)} %add_multiply_fusion.4, f32[16,30,284]{2,1,0:T(8,128)S(1)} %get-tuple-element.240, f32[16,30,284]{2,1,0:T(8,128)S(1)} %get-tuple-element.239, f32[16,30,284]{2,1,0:T(8,128)S(1)} %get-tuple-element.238, f32[16,30,284]{2,1,0:T(8,128)S(1)} %get-tuple-element.237, ...), kind=kLoop, calls=%fused_computation.18 | loop fusion | flops 2044800 | bytes 3819232 | tf_op jit(solution)/shard_map/add | solution.py:151
  51.4 0.8 %multiply_add_fusion.2 = f32[16,30,284]{2,1,0:T(8,128)S(1)} fusion(f32[16,30,284]{2,1,0:T(8,128)S(1)} %broadcast_multiply_fusion, f32[16,30,284]{2,1,0:T(8,128)S(1)} %get-tuple-element.240, f32[16,30,284]{2,1,0:T(8,128)S(1)} %get-tuple-element.239, f32[16,30,284]{2,1,0:T(8,128)S(1)} %get-tuple-element.238, f32[16,30,284]{2,1,0:T(8,128)S(1)} %get-tuple-element.237, ...), kind=kLoop, calls=%fused_computation.16 | loop fusion | flops 1772160 | bytes 3273952 | tf_op jit(solution)/shard_map/add | solution.py:148
  52.9 0.8 %multiply_add_fusion.1 = f32[16,30,284]{2,1,0:T(8,128)S(1)} fusion(f32[16,30,284]{2,1,0:T(8,128)S(1)} %add_multiply_fusion.2, f32[16,30,284]{2,1,0:T(8,128)S(1)} %get-tuple-element.240, f32[16,30,284]{2,1,0:T(8,128)S(1)} %get-tuple-element.239, f32[16,30,284]{2,1,0:T(8,128)S(1)} %get-tuple-element.238, f32[16,30,284]{2,1,0:T(8,128)S(1)} %get-tuple-element.237, ...), kind=kLoop, calls=%fused_computation.14 | loop fusion | flops 1772160 | bytes 3273952 | tf_op jit(solution)/shard_map/add | solution.py:148
  54.5 0.8 %multiply_add_fusion = f32[16,30,284]{2,1,0:T(8,128)S(1)} fusion(f32[16,30,284]{2,1,0:T(8,128)S(1)} %add_multiply_fusion.1, f32[16,30,284]{2,1,0:T(8,128)S(1)} %get-tuple-element.240, f32[16,30,284]{2,1,0:T(8,128)S(1)} %get-tuple-element.239, f32[16,30,284]{2,1,0:T(8,128)S(1)} %get-tuple-element.238, f32[16,30,284]{2,1,0:T(8,128)S(1)} %get-tuple-element.237, ...), kind=kLoop, calls=%fused_computation.12 | loop fusion | flops 1772160 | bytes 3273952 | tf_op jit(solution)/shard_map/add | solution.py:148
  56.3 0.7 %pad_maximum_fusion.4 = f32[2,16,16,128]{3,2,1,0:T(8,128)} fusion(f32[1,16,16,128]{3,2,1,0:T(8,128)S(1)} %get-tuple-element.247, f32[1,16,16,128]{3,2,1,0:T(8,128)S(1)} %get-tuple-element.246), kind=kLoop, calls=%fused_computation.40 | loop fusion | flops 65536 | bytes 524288 | tf_op jit(solution)/shard_map/stack | solution.py:271
  58.4 11.0 %all_gather.3 = f32[8,8,16]{2,1,0:T(8,128)S(1)} all-gather(f32[1,8,16]{2,1,0:T(8,128)S(1)} %add.4716), channel_id=1, replica_groups=mesh['gx'=4,'gy'=8] {'gy'}, dimensions={0}, use_global_device_ids=true | all-gather | bytes 4608 | tf_op jit(solution)/shard_map/all_gather | solution.py:300
  (239 shorter events, 15.9 us)
Async XLA Ops:
  0.6 14.8 %copy-start = (f32[2,16,16,128]{3,2,1,0:T(8,128)S(1)}, f32[2,16,16,128]{3,2,1,0:T(8,128)}, u32[]{:S(2)}) copy-start(f32[2,16,16,128]{3,2,1,0:T(8,128)} %param.8) | copy-start | bytes 786436
  5.4 12.9 %collective-permute-start = (f32[53,7,128]{2,1,0:T(8,128)S(1)}, f32[53,7,128]{2,1,0:T(8,128)S(1)}, u32[]{:S(2)}, u32[]{:S(2)}) collective-permute-start(f32[53,7,128]{2,1,0:T(8,128)S(1)} %get-tuple-element.286), channel_id=1, source_target_pairs={{0,8},{8,16},{16,24},{1,9},{9,17},{17,25},{2,10},{10,18},{18,26},{... | collective-permute-start | bytes 569864 | tf_op jit(solution)/shard_map/ppermute | solution.py:178
  10.3 8.7 %collective-permute-start.1 = (f32[53,7,128]{2,1,0:T(8,128)S(1)}, f32[53,7,128]{2,1,0:T(8,128)S(1)}, u32[]{:S(2)}, u32[]{:S(2)}) collective-permute-start(f32[53,7,128]{2,1,0:T(8,128)S(1)} %get-tuple-element.287), channel_id=1, source_target_pairs={{8,0},{16,8},{24,16},{9,1},{17,9},{25,17},{10,2},{18,10},{26,18},{... | collective-permute-start | bytes 569864 | tf_op jit(solution)/shard_map/ppermute | solution.py:178
  11.7 5.7 %copy-start.1 = (f32[16,16,128]{2,1,0:T(8,128)S(1)}, f32[16,16,128]{2,1,0:T(8,128)}, u32[]{:S(2)}) copy-start(f32[16,16,128]{2,1,0:T(8,128)} %param.9) | copy-start | bytes 393220
  14.3 3.2 %copy-start.2 = (f32[2,16,128]{2,1,0:T(8,128)S(1)}, f32[2,16,128]{2,1,0:T(8,128)}, u32[]{:S(2)}) copy-start(f32[2,16,128]{2,1,0:T(8,128)} %param.10) | copy-start | bytes 49156
  14.3 3.2 %copy-start.5 = (s32[16,128]{1,0:T(8,128)S(1)}, s32[16,128]{1,0:T(8,128)}, u32[]{:S(2)}) copy-start(s32[16,128]{1,0:T(8,128)} %param.12) | copy-start | bytes 24580
  15.4 2.8 %copy-start.6 = (s32[16,128]{1,0:T(8,128)S(1)}, s32[16,128]{1,0:T(8,128)}, u32[]{:S(2)}) copy-start(s32[16,128]{1,0:T(8,128)} %param.13) | copy-start | bytes 24580
  15.4 3.6 %copy-start.7 = (f32[1,16]{1,0:T(1,128)S(1)}, f32[1,16]{1,0:T(1,128)}, u32[]{:S(2)}) copy-start(f32[1,16]{1,0:T(1,128)} %param.11) | copy-start | bytes 196
  19.0 8.6 %collective-permute-start.5 = (f32[3,16]{1,0:T(4,128)S(1)}, f32[3,16]{1,0:T(4,128)S(1)}, u32[]{:S(2)}, u32[]{:S(2)}) collective-permute-start(f32[3,16]{1,0:T(4,128)S(1)} %pad_maximum_fusion.17), channel_id=1, source_target_pairs={{0,7},{1,0},{2,1},{3,2},{4,3},{5,4},{6,5},{7,6},{8,15},{9,8},{10,9... | collective-permute-start | bytes 584 | tf_op jit(solution)/shard_map/ppermute | solution.py:21
  19.9 5.8 %collective-permute-start.4 = (f32[3,16]{1,0:T(4,128)S(1)}, f32[3,16]{1,0:T(4,128)S(1)}, u32[]{:S(2)}, u32[]{:S(2)}) collective-permute-start(f32[3,16]{1,0:T(4,128)S(1)} %pad_maximum_fusion.17), channel_id=1, source_target_pairs={{0,1},{1,2},{2,3},{3,4},{4,5},{5,6},{6,7},{7,0},{8,9},{9,10},{10,1... | collective-permute-start | bytes 584 | tf_op jit(solution)/shard_map/ppermute | solution.py:18
  20.9 17.8 %collective-permute-start.3 = (f32[52,30,7]{0,1,2:T(8,128)S(1)}, f32[52,30,7]{0,1,2:T(8,128)S(1)}, u32[]{:S(2)}, u32[]{:S(2)}) collective-permute-start(f32[52,30,7]{0,1,2:T(8,128)S(1)} %pad_maximum_fusion.6), channel_id=1, source_target_pairs={{1,0},{2,1},{3,2},{4,3},{5,4},{6,5},{7,6},{9,8},{10,9},{11,10},{12... | collective-permute-start | bytes 131048 | tf_op jit(solution)/shard_map/ppermute | solution.py:178
  22.2 15.6 %collective-permute-start.2 = (f32[52,30,7]{0,1,2:T(8,128)S(1)}, f32[52,30,7]{0,1,2:T(8,128)S(1)}, u32[]{:S(2)}, u32[]{:S(2)}) collective-permute-start(f32[52,30,7]{0,1,2:T(8,128)S(1)} %pad_maximum_fusion.5), channel_id=1, source_target_pairs={{0,1},{1,2},{2,3},{3,4},{4,5},{5,6},{6,7},{8,9},{9,10},{10,11},{11... | collective-permute-start | bytes 131048 | tf_op jit(solution)/shard_map/ppermute | solution.py:178
  25.8 4.0 %collective-permute-start.6 = (f32[3,16]{1,0:T(4,128)S(1)}, f32[3,16]{1,0:T(4,128)S(1)}, u32[]{:S(2)}, u32[]{:S(2)}) collective-permute-start(f32[3,16]{1,0:T(4,128)S(1)} %collective-permute-done.4), channel_id=1, source_target_pairs={{0,1},{1,2},{2,3},{3,4},{4,5},{5,6},{6,7},{7,0},{8,9},{9,10},{10,1... | collective-permute-start | bytes 584 | tf_op jit(solution)/shard_map/ppermute | solution.py:18
  27.7 2.1 %collective-permute-start.7 = (f32[3,16]{1,0:T(4,128)S(1)}, f32[3,16]{1,0:T(4,128)S(1)}, u32[]{:S(2)}, u32[]{:S(2)}) collective-permute-start(f32[3,16]{1,0:T(4,128)S(1)} %collective-permute-done.5), channel_id=1, source_target_pairs={{0,7},{1,0},{2,1},{3,2},{4,3},{5,4},{6,5},{7,6},{8,15},{9,8},{10,9... | collective-permute-start | bytes 584 | tf_op jit(solution)/shard_map/ppermute | solution.py:21
  29.7 3.9 %collective-permute-start.8 = (f32[3,16]{1,0:T(4,128)S(1)}, f32[3,16]{1,0:T(4,128)S(1)}, u32[]{:S(2)}, u32[]{:S(2)}) collective-permute-start(f32[3,16]{1,0:T(4,128)S(1)} %collective-permute-done.6), channel_id=1, source_target_pairs={{0,1},{1,2},{2,3},{3,4},{4,5},{5,6},{6,7},{7,0},{8,9},{9,10},{10,1... | collective-permute-start | bytes 584 | tf_op jit(solution)/shard_map/ppermute | solution.py:18
  29.8 4.1 %collective-permute-start.9 = (f32[3,16]{1,0:T(4,128)S(1)}, f32[3,16]{1,0:T(4,128)S(1)}, u32[]{:S(2)}, u32[]{:S(2)}) collective-permute-start(f32[3,16]{1,0:T(4,128)S(1)} %collective-permute-done.7), channel_id=1, source_target_pairs={{0,7},{1,0},{2,1},{3,2},{4,3},{5,4},{6,5},{7,6},{8,15},{9,8},{10,9... | collective-permute-start | bytes 584 | tf_op jit(solution)/shard_map/ppermute | solution.py:21
  33.6 3.9 %collective-permute-start.10 = (f32[3,16]{1,0:T(4,128)S(1)}, f32[3,16]{1,0:T(4,128)S(1)}, u32[]{:S(2)}, u32[]{:S(2)}) collective-permute-start(f32[3,16]{1,0:T(4,128)S(1)} %collective-permute-done.8), channel_id=1, source_target_pairs={{0,1},{1,2},{2,3},{3,4},{4,5},{5,6},{6,7},{7,0},{8,9},{9,10},{10,1... | collective-permute-start | bytes 584 | tf_op jit(solution)/shard_map/ppermute | solution.py:18
  40.7 3.0 %copy-start.3 = (f32[284]{0:T(512)S(1)}, f32[284]{0:T(512)}, u32[]{:S(2)}) copy-start(f32[284]{0:T(512)} %constant.96.clone.1) | copy-start | bytes 3412
  40.7 3.0 %copy-start.4 = (f32[284]{0:T(512)S(1)}, f32[284]{0:T(512)}, u32[]{:S(2)}) copy-start(f32[284]{0:T(512)} %constant.94.clone.1) | copy-start | bytes 3412
